TPU v7x, 512 devices: a whole 4x4x16 slice. The times are simulated.
512 devices in a mesh: dp: 32 (over z, core), seq: 16 (over y, x).
Axes of the slice: x: 4, y: 4, z: 16, core: 2. Of those that a mesh axis runs over, the one named last changes fastest.
Arguments:
- mixer_in: bfloat16 [131072, 2816], P(('dp', 'seq')), parts along dimension 0, may hold values from -92 to 92
- gate_input: bfloat16 [131072, 2560], P(('dp', 'seq')), parts along dimension 0, may hold values from -6 to 6
- step_raw: bfloat16 [131072, 40], P(('dp', 'seq')), parts along dimension 0, may hold values from -6 to 6
- lengths: int32 [96], P('dp'), parts along dimension 0, may hold values from 1 to 2048, 4096 in all
- deal_order: int32 [512], P('dp'), parts along dimension 0, may hold values from 0 to 15, as said below
- conv_weight: float32 [4, 2816], replicated, may hold values from -3 to 3
- conv_bias: float32 [2816], replicated, may hold values from -3 to 3
- step_bias: float32 [40], replicated, may hold values from -4 to -1
- decay_rate: float32 [40], replicated, may hold values from 0.01 to 2
- skip_gain: float32 [40], replicated, may hold values from 0.5 to 1.5
- norm_gain: float32 [2560], replicated, may hold values from 0.5 to 1.5
Outputs:
- mixed_out: bfloat16 [131072, 2560], P(('dp', 'seq')), parts along dimension 0
- final_states: float32 [96, 2560, 128], P('dp', 'seq'), parts along dimension 0
There are 32 independent parts, one for each index of `dp`. A program takes and returns all parts, laid end to end along the dimension named above; an argument that names none is the same for every part. Nothing has to cross between parts.
Inputs may be any that keep to these rules, and one draw needn't show every extreme that they name: The prompt lengths sum to 4096 and the longest is exactly 2048. `deal_order`: every sequence stretch stands in exactly one dealt slot.
All inputs are finite; a program needn't handle non-finite values.
Results may differ from a plain program's by a relative error of at most 0.005.
Values may be sent and summed in bfloat16 or wider, within the bound.
No kernel may reach another device: no remote copies, remote signals or barrier semaphores. Data moves between devices by JAX's collectives and lax.ppermute only.
A program may use at most 128 MiB of HBM per device.

v0:
```python
import jax
import jax.numpy as jnp
from jax import lax
from jax.sharding import PartitionSpec as P

HEADS = 40
HEAD_DIM = 64
STATE = 128
KERNEL = 4
STRETCH = 256
DOCS = 3
INNER = 2560
CHANNELS = 2816


def doc_index(ends, positions):
    return jnp.sum((ends[None, :] <= positions[:, None]).astype(jnp.int32), axis=1)


def body(
    mixer_in,
    gate_input,
    step_raw,
    lengths,
    deal_order,
    conv_weight,
    conv_bias,
    step_bias,
    decay_rate,
    skip_gain,
    norm_gain,
):
    myself = lax.axis_index("seq")
    local_rows = mixer_in.shape[0]
    stretches_here = local_rows // STRETCH
    stretch_total = deal_order.shape[0]
    ends = jnp.cumsum(lengths)
    all_stretches = jnp.arange(stretch_total, dtype=jnp.int32)
    my_stretches = lax.dynamic_slice_in_dim(deal_order, myself * stretches_here, stretches_here)
    lane = jnp.arange(STRETCH, dtype=jnp.int32)
    own_doc = doc_index(
        ends, (my_stretches[:, None] * STRETCH + lane[None, :]).reshape(-1)
    ).reshape(stretches_here, STRETCH)
    prev_own = jnp.where(my_stretches > 0, doc_index(ends, my_stretches * STRETCH - 1), -1)
    blocks_in = mixer_in.reshape(stretches_here, STRETCH, CHANNELS)
    tails = blocks_in[:, STRETCH - (KERNEL - 1) :, :]
    step_blocks = step_raw.reshape(stretches_here, STRETCH, HEADS)
    step = jax.nn.softplus(step_blocks.astype(jnp.float32) + step_bias)
    log_decay = -decay_rate * step
    all_tails, all_steps = (
        lax.all_gather(tails, "seq", axis=0, tiled=True),
        lax.all_gather(step_blocks, "seq", axis=0, tiled=True),
    )
    totals = jnp.sum(
        -decay_rate * jax.nn.softplus(all_steps.astype(jnp.float32) + step_bias), axis=1
    )
    slot_map = (deal_order[:, None] == all_stretches[None, :]).astype(jnp.float32)
    packed_totals = jnp.dot(slot_map.T, totals, precision=lax.Precision.HIGHEST)
    prefix = jnp.cumsum(packed_totals, axis=0)
    base = jnp.concatenate([jnp.zeros((1, HEADS), jnp.float32), prefix[:-1]], 0)
    pick_own = (my_stretches[:, None] == all_stretches[None, :]).astype(jnp.float32)
    base_own = jnp.dot(pick_own, base, precision=lax.Precision.HIGHEST)
    running = base_own[:, None, :] + jnp.cumsum(log_decay, axis=1)
    prev_pick = (deal_order[None, :] == my_stretches[:, None] - 1).astype(jnp.bfloat16)
    prev_rows = jnp.einsum(
        "is,skc->ikc", prev_pick, all_tails, preferred_element_type=jnp.float32
    ).astype(jnp.bfloat16)
    extended = jnp.concatenate([prev_rows, blocks_in], 1)
    lead = (
        my_stretches[:, None] * STRETCH
        - (KERNEL - 1)
        + jnp.arange(KERNEL - 1, dtype=jnp.int32)[None, :]
    ).reshape(-1)
    ext_doc = jnp.concatenate(
        [doc_index(ends, lead).reshape(stretches_here, KERNEL - 1), own_doc], 1
    )
    accum = jnp.zeros((stretches_here, STRETCH, CHANNELS), jnp.float32) + conv_bias
    for offset in range(KERNEL):
        keep = (ext_doc[:, offset : offset + STRETCH] == own_doc).astype(jnp.float32)
        accum = (
            accum
            + conv_weight[offset]
            * extended[:, offset : offset + STRETCH, :].astype(jnp.float32)
            * keep[..., None]
        )
    mixed = jax.nn.silu(accum).astype(jnp.bfloat16)
    values = mixed[..., :INNER]
    input_map = mixed[..., INNER : INNER + STATE]
    output_map = mixed[..., INNER + STATE :]
    scaled = (values.astype(jnp.float32) * jnp.repeat(step, HEAD_DIM, axis=2)).astype(jnp.bfloat16)
    end_weight = jnp.exp(
        jnp.where((own_doc == own_doc[:, -1:])[..., None], running[:, -1:, :] - running, -jnp.inf)
    )
    weighted = (scaled.astype(jnp.float32) * jnp.repeat(end_weight, HEAD_DIM, axis=2)).astype(
        jnp.bfloat16
    )
    states = jnp.einsum("isk,isn->ikn", weighted, input_map, preferred_element_type=jnp.float32)
    source_pick = (deal_order[:, None] == all_stretches[None, :]).astype(jnp.float32)
    source_end = jnp.dot(source_pick, prefix, precision=lax.Precision.HIGHEST)
    source_doc = doc_index(ends, deal_order * STRETCH + STRETCH - 1)
    allowed = (deal_order[None, :] < my_stretches[:, None]) & (
        source_doc[None, :] == prev_own[:, None]
    )
    spans = jnp.exp(
        jnp.where(allowed[..., None], base_own[:, None, :] - source_end[None, :, :], -jnp.inf)
    )
    state_in = jnp.einsum(
        "ick,ckn->ikn",
        jnp.repeat(spans, HEAD_DIM, axis=2),
        lax.all_gather(states, "seq", axis=0, tiled=True),
        precision=lax.Precision.HIGHEST,
    )
    later = lane[:, None] >= lane[None, :]
    direct_gain = jnp.repeat(skip_gain, HEAD_DIM)[None, :]

    def stretch_out(inputs):
        values_c, scaled_c, keys_c, queries_c, running_c, doc_c, base_c, prev_c, state_c = inputs
        scores = jnp.dot(queries_c, keys_c.T, preferred_element_type=jnp.float32)
        same = (doc_c[:, None] == doc_c[None, :]) & later
        spans = running_c.T[:, :, None] - running_c.T[:, None, :]
        mixing = (scores[None] * jnp.exp(jnp.where(same[None], spans, -jnp.inf))).astype(
            jnp.bfloat16
        )
        within = jnp.einsum(
            "hts,shp->thp",
            mixing,
            scaled_c.reshape(STRETCH, HEADS, HEAD_DIM),
            preferred_element_type=jnp.float32,
        ).reshape(STRETCH, INNER)
        readout = jnp.dot(
            queries_c, state_c.astype(jnp.bfloat16).T, preferred_element_type=jnp.float32
        )
        carry_weight = jnp.exp(
            jnp.where((doc_c == prev_c)[:, None], running_c - base_c[None, :], -jnp.inf)
        )
        return (
            within
            + readout * jnp.repeat(carry_weight, HEAD_DIM, axis=1)
            + values_c.astype(jnp.float32) * direct_gain
        )

    outputs = lax.map(
        stretch_out,
        (values, scaled, input_map, output_map, running, own_doc, base_own, prev_own, state_in),
    )
    gated = outputs.reshape(local_rows, INNER) * jax.nn.silu(gate_input.astype(jnp.float32))
    normed = gated * lax.rsqrt(jnp.mean(gated * gated, axis=1, keepdims=True) + 1e-05) * norm_gain
    mixed_out = normed.astype(jnp.bfloat16)
    slot_numbers = jnp.arange(stretches_here, dtype=jnp.int32)

    def one_doc(document):
        last = lax.dynamic_index_in_dim(ends, document, keepdims=False) - 1
        owner = last // STRETCH
        match = my_stretches == owner
        slot = jnp.sum(jnp.where(match, slot_numbers, 0))

        def present():
            within_pos = last - owner * STRETCH
            running_c = lax.dynamic_index_in_dim(running, slot, keepdims=False)
            running_e = lax.dynamic_index_in_dim(running_c, within_pos, keepdims=False)
            doc_c = lax.dynamic_index_in_dim(own_doc, slot, keepdims=False)
            scaled_c = lax.dynamic_index_in_dim(scaled, slot, keepdims=False)
            keys_c = lax.dynamic_index_in_dim(input_map, slot, keepdims=False)
            base_c = lax.dynamic_index_in_dim(base_own, slot, keepdims=False)
            prev_c = lax.dynamic_index_in_dim(prev_own, slot, keepdims=False)
            state_c = lax.dynamic_index_in_dim(state_in, slot, keepdims=False)
            weight = jnp.exp(
                jnp.where((doc_c == document)[:, None], running_e[None, :] - running_c, -jnp.inf)
            )
            final_weighted = (
                scaled_c.astype(jnp.float32) * jnp.repeat(weight, HEAD_DIM, axis=1)
            ).astype(jnp.bfloat16)
            part = jnp.dot(final_weighted.T, keys_c, preferred_element_type=jnp.float32)
            carry_weight = jnp.exp(jnp.where(prev_c == document, running_e - base_c, -jnp.inf))
            return part + jnp.repeat(carry_weight, HEAD_DIM)[:, None] * state_c

        def absent():
            return jnp.zeros((INNER, STATE), jnp.float32)

        return lax.cond(jnp.any(match), present, absent)

    every_doc = jnp.transpose(lax.map(one_doc, jnp.arange(DOCS, dtype=jnp.int32)), (1, 0, 2))
    kept = lax.psum_scatter(
        every_doc.astype(jnp.bfloat16), "seq", scatter_dimension=0, tiled=True
    ).astype(jnp.float32)
    final_states = jnp.transpose(kept, (1, 0, 2))
    return (mixed_out, final_states)


def solution(mesh):
    return jax.shard_map(
        body,
        mesh=mesh,
        in_specs=(
            P(("dp", "seq"), None),
            P(("dp", "seq"), None),
            P(("dp", "seq"), None),
            P("dp"),
            P("dp"),
            P(),
            P(),
            P(),
            P(),
            P(),
            P(),
        ),
        out_specs=(P(("dp", "seq"), None), P("dp", "seq", None)),
        check_vma=False,
    )
```

profile of v0, /device:TPU:2, one launch (start us, length us, event | category | flops | bytes accessed | tf_op | source)
XLA Modules:
  0.0 391.7 jit_solution(15185379277083827339)
XLA Ops:
  7.2 0.7 neg.23
  7.9 26.9 %all-gather = bf16[4096,40]{0,1:T(8,128)(2,1)S(1)} all-gather(bf16[256,40]{0,1:T(8,128)(2,1)} %param.17), channel_id=2, replica_groups=mesh['dp'=32,'seq'=16] {'seq'}, dimensions={0}, use_global_device_ids=true | all-gather | bytes 348160 | tf_op jit(solution)/shard_map/all_gather | solution.py:52
  34.8 0.8 multiply_bitcast_fusion
  35.7 0.6 reduce-window.11
  36.3 0.2 slice_reduce_fusion
  36.5 1.2 dynamic_slice.62
  39.0 0.8 reduce-window.10
  39.9 0.2 convert_reduce_fusion.2
  40.1 0.6 slice.90
  40.8 0.8 slice.76
  41.6 21.6 %all_gather.9 = bf16[16,3,2816]{2,1,0:T(4,128)(2,1)S(1)} all-gather(bf16[1,3,2816]{2,1,0:T(4,128)(2,1)S(1)} %slice.76), channel_id=1, replica_groups=mesh['dp'=32,'seq'=16] {'seq'}, dimensions={0}, use_global_device_ids=true | all-gather | bytes 287232 | tf_op jit(solution)/shard_map/all_gather | solution.py:51
  63.2 0.8 fusion.32
  64.1 1.1 slice_reduce_fusion.5
  65.1 0.2 broadcast_in_dim.178
  65.4 2.1 copy.73
  67.5 0.6 fusion.55
  68.8 0.2 copy.93
  69.0 0.6 fusion.30
  69.6 0.2 fusion.45
  70.1 0.8 fusion.42
  70.8 0.1 broadcast.161
  70.9 0.1 add_bitcast_fusion
  71.1 0.6 slice_reduce_fusion.1
  72.3 0.6 broadcast_compare_fusion.1
  73.0 0.1 fusion.38
  73.1 0.2 broadcast_in_dim.184
  73.3 2.1 copy.78
  75.5 5.9 %multiply_convert_fusion.2 = bf16[1,256,2816]{2,1,0:T(8,128)(2,1)S(1)} fusion(bf16[256,2816]{1,0:T(8,128)(2,1)} %param.15, bf16[1,3,2816]{2,1,0:T(4,128)(2,1)S(1)} %copy.108, bf16[1,256,2816]{2,1,0:T(8,128)(2,1)} %bitcast.153, f32[2816]{0:T(1024)S(1)} %get-tuple-element.357, f32[256]{0:T(256)S(1)} %bitcast.173, f32[2816]{0:T(1024)S(1)} %get-tuple-element.358, ...), kind=kLoop, calls=%fused_computation.33 | loop fusion | flops 20905984 | bytes 4401664 | tf_op jit(solution)/shard_map/convert_element_type | solution.py:86
  81.4 0.4 fusion.17
  81.8 1.9 copy-done.1
  83.7 1.8 fusion.25
  85.5 0.2 reduce-scatter.2.cloned.1.call-start
  85.8 1.4 copy.74
  87.3 0.7 compare_and_fusion
  88.0 0.2 fusion.28
  88.2 146.0 %all-gather.4.cloned.1.call-done = f32[40960,128]{1,0:T(8,128)} async-done(((f32[2560,128]{1,0:T(8,128)}), f32[40960,128]{1,0:T(8,128)}) %all-gather.4.cloned.1.call-update) | async-done | bytes 20971536 | tf_op jit(solution)/shard_map/all_gather | solution.py:110
  234.4 38.9 %fusion.6 = f32[2560,1,128]{2,1,0:T(1,128)S(1)} fusion(f32[16,2560,1]{0,2,1:T(1,128)S(1)} %bitcast.151, f32[16,2560,128]{2,1,0:T(8,128)} %bitcast.147), kind=kOutput, calls=%fused_computation.15 | convolution fusion | flops 62914560 | bytes 22446080 | tf_op jit(solution)/shard_map/ick,ckn->ikn/dot_general | solution.py:107
  273.3 20.2 %while.17 = (s32[]{:T(128)}, bf16[3,2560,128]{2,1,0:T(8,128)(2,1)}, s32[3]{0:T(128)S(1)}, s32[3]{0:T(128)S(1)}, s32[1]{0:T(128)}, /*index=5*/bf16[1,256,2560]{1,...) while((s32[]{:T(128)}, bf16[3,2560,128]{2,1,0:T(8,128)(2,1)}, ...), condition=%wide.region_13.14_spmd, body=%wide.region_10.13_spmd.sunk | while | flops 170742112 | bytes 7442075 | solution.py:182
  273.3 0.6 dynamic_slice.66
  275.8 0.6 dynamic_slice.67
  277.7 4.0 %conditional.2 = (bf16[1,2560,128]{2,1,0:T(8,128)(2,1)S(1)}) conditional(s32[]{:T(128)} %bitcast.143, () %tuple.66, (bf16[1,256,2560]{1,2,0:T(8,128)(2,1)}, s32[]{:T(128)}, s32[1,256]{1,0:T(1,128)S(1)}, s32[]{:T(128)}, s32[]{:T(128)}, /*index=5*/f32[1,256,40]{1,2,0:T(8,128)S(1)}, bf16[1,256,128]{2,1,0:T(8,128)(2,1)S(1)}, s32[1]{0:T(128)}, ...), branch_computations={%region_11.11_spmd, %region_12.12_spmd} | conditional | flops 170742096 | bytes 6130356 | solution.py:180
  277.7 0.2 dynamic-slice_reduce_fusion
  277.9 0.7 compare_reduce_fusion
  278.6 1.7 fusion.1
  281.1 0.5 fusion
  281.7 0.9 constant_dynamic-update-slice_fusion.2
  282.5 0.6 dynamic_slice.66
  285.1 0.6 dynamic_slice.67
  287.0 0.1 conditional.2
  287.1 0.9 constant_dynamic-update-slice_fusion.2
  288.0 0.6 dynamic_slice.66
  290.5 0.6 dynamic_slice.67
  292.4 0.1 conditional.2
  292.5 0.9 constant_dynamic-update-slice_fusion.2
  293.4 0.1 fusion.34
  293.5 1.1 fusion.36
  294.6 5.1 %fusion.8 = f32[40,64,256]{2,1,0:T(8,128)} fusion(bf16[256,40,64]{0,2,1:T(8,128)(2,1)} %bitcast.28, f32[40,256]{1,0:T(8,128)S(1)} %bitcast.154, f32[256,256]{1,0:T(8,128)S(1)} %fusion.36, pred[256,256]{1,0:T(8,128)(4,1)S(1)} %fusion.34), kind=kOutput, calls=%fused_computation.18 | convolution fusion | flops 346030080 | bytes 4300800 | tf_op jit(solution)/shard_map/while/body/eval_jaxpr/hts,shp->thp/dot_general | solution.py:124
  299.7 3.2 copy.80
  303.0 1.7 broadcast_in_dim.192
  304.7 3.4 copy.79
  308.2 4.6 %multiply_reduce_fusion = (f32[256]{0:T(256)S(1)}, f32[256,2560]{1,0:T(8,128)S(1)}) fusion(bf16[256,2560]{1,0:T(8,128)(2,1)S(1)} %copy-done.8, f32[2560]{0:T(1024)S(1)} %mul.239, bf16[1,256,2816]{2,1,0:T(8,128)(2,1)} %copy-done.2, f32[256,2560]{1,0:T(8,128)} %copy.80, f32[256,2560]{1,0:T(8,128)} %copy.79, f32[2560,128]{1,0:T(8,128)S(1)} %bitcast.146), kind=kOutput, calls=%fused_computation.40 | convolution fusion | flops 176619264 | bytes 11873280 | tf_op jit(solution)/shard_map/while/body/eval_jaxpr/dot_general | solution.py:130
  312.9 1.3 multiply_convert_fusion.3
  314.2 69.0 %reduce-scatter.2.cloned.1.call-done = bf16[160,3,128]{2,0,1:T(8,128)(2,1)} async-done(((bf16[2560,3,128]{2,0,1:T(8,128)(2,1)}), bf16[160,3,128]{2,0,1:T(8,128)(2,1)}) %reduce-scatter.2.cloned.1.call-update) | async-done | bytes 122896 | tf_op jit(solution)/shard_map/reduce_scatter | solution.py:183
  383.3 1.6 convert_bitcast_fusion.2
  (51 shorter events, 1.5 us)
Async XLA Ops:
  7.2 227.1 %all-gather.4.cloned.1.call-start = ((), (), s32[]{:S(2)}) async-start(), calls=%async_computation.2 | async-start | bytes 22282240 | tf_op jit(solution)/shard_map/all_gather | solution.py:110
  65.4 3.7 copy-start.6
  67.5 2.1 copy-start.5
  73.3 2.1 copy-start.4
  75.5 5.9 %copy-start = (f32[1,256,2560]{2,1,0:T(8,128)S(1)}, f32[1,256,2560]{2,1,0:T(8,128)}, u32[]{:S(2)}) copy-start(f32[1,256,2560]{2,1,0:T(8,128)} %copy.73) | copy-start | bytes 7864324
  81.4 153.0 %copy-start.2 = (bf16[1,256,2816]{2,1,0:T(8,128)(2,1)}, bf16[1,256,2816]{2,1,0:T(8,128)(2,1)S(1)}, u32[]{:S(2)}) copy-start(bf16[1,256,2816]{2,1,0:T(8,128)(2,1)S(1)} %multiply_convert_fusion.2) | copy-start | bytes 4325380
  81.4 2.3 copy-start.1
  85.5 297.7 %reduce-scatter.2.cloned.1.call-start = ((), (), s32[]{:S(2)}) async-start(), calls=%async_computation.1 | async-start | bytes 2088960 | tf_op jit(solution)/shard_map/reduce_scatter | solution.py:183
  304.7 3.4 copy-start.7
  304.7 3.5 copy-start.8
  308.2 4.7 %copy-start.3 = (f32[2560]{0:T(1024)S(1)}, f32[2560]{0:T(1024)}, u32[]{:S(2)}) copy-start(f32[2560]{0:T(1024)} %param.25) | copy-start | bytes 30724
Sparse Core Ops, SparseCore 0:
  85.7 148.5 all-gather.3
  293.6 89.6 reduce-scatter.1
where the time goes:
time: 393 us; the launch traced here: 392 us
  waiting for transfers between devices  215 us (55%)
  matrix products  54 us (14%)
  blocking collectives  48.5 us (12%)
  local copies, waits for them, and re-layouts  28.5 us (7%)
  other arithmetic  18 us (5%)
  between operations  17 us (4%)
  loops' own time  10.3 us (3%)
    all_gather x1, waiting for transfers between devices, body(): lax.all_gather(states, 'seq', axis=0, tiled=True)  146 us
    reduce_scatter x1, waiting for transfers between devices, body(): lax.psum_scatter(every_doc.astype(jnp.bfloat16), 'seq', scatter_dimension...  69 us
    dot_general x1, matrix products, body(): jnp.einsum('ick,ckn->ikn', jnp.repeat(spans, HEAD_DIM, axis=2), lax.all_g...  38.9 us
    all_gather x1, blocking collectives, body(): lax.all_gather(step_blocks, 'seq', axis=0, tiled=True)  26.9 us
    all_gather x1, blocking collectives, body(): lax.all_gather(tails, 'seq', axis=0, tiled=True)  21.6 us
    another operation x1, loops' own time, body(): lax.map(one_doc, jnp.arange(DOCS, dtype=jnp.int32))  9.57 us
  transfers between devices with their start and end apart: 2, of which 2 were waited for; matrix products, arithmetic and copies ran while one was open for 6% of the time, Pallas kernels for 0%

commit v1 on v0

--- a/solution.py
+++ b/solution.py
@@ -48,7 +48,9 @@
     step = jax.nn.softplus(step_blocks.astype(jnp.float32) + step_bias)
     log_decay = -decay_rate * step
     all_tails, all_steps = (
-        lax.all_gather(tails, "seq", axis=0, tiled=True),
+        jnp.concatenate(
+            lax.all_to_all(jnp.stack([tails] * lax.axis_size("seq")), "seq", 0, 0), axis=0
+        ),
         lax.all_gather(step_blocks, "seq", axis=0, tiled=True),
     )
     totals = jnp.sum(

time: 393 us -> 378 us (0.962)
  blocking collectives: 48.5 us -> 23.8 us
  starting transfers between devices: 0.26 us -> 9.48 us
    all_gather x1 -> x0, blocking collectives: 21.6 us -> none  [body(): lax.all_gather(tails, 'seq', axis=0, tiled=True)]
    all_to_all x0 -> x1, starting transfers between devices: none -> 9.22 us  [body(): lax.all_to_all(jnp.stack([tails] * lax.axis_size('seq')), 'seq', 0, 0)]
  transfers between devices with their start and end apart: 2 -> 3, of which waited for: 2 -> 2; matrix products, arithmetic and copies ran while one was open for 6% -> 10% of each run, Pallas kernels for 0% -> 0%
where the time goes in v1:
time: 378 us; the launch traced here: 377 us
  waiting for transfers between devices  215 us (57%)
  matrix products  53.4 us (14%)
  local copies, waits for them, and re-layouts  27.8 us (7%)
  blocking collectives  23.8 us (6%)
  other arithmetic  20.3 us (5%)
  between operations  17 us (4%)
  loops' own time  10.3 us (3%)
  starting transfers between devices  9.48 us (3%)
    all_gather x1, waiting for transfers between devices, body(): lax.all_gather(states, 'seq', axis=0, tiled=True)  146 us
    reduce_scatter x1, waiting for transfers between devices, body(): lax.psum_scatter(every_doc.astype(jnp.bfloat16), 'seq', scatter_dimension...  69 us
    dot_general x1, matrix products, body(): jnp.einsum('ick,ckn->ikn', jnp.repeat(spans, HEAD_DIM, axis=2), lax.all_g...  38.9 us
    all_gather x1, blocking collectives, body(): lax.all_gather(step_blocks, 'seq', axis=0, tiled=True)  23.8 us
    another operation x1, loops' own time, body(): lax.map(one_doc, jnp.arange(DOCS, dtype=jnp.int32))  9.58 us
    all_to_all x1, starting transfers between devices, body(): lax.all_to_all(jnp.stack([tails] * lax.axis_size('seq')), 'seq', 0, 0)  9.22 us
  transfers between devices with their start and end apart: 3, of which 2 were waited for; matrix products, arithmetic and copies ran while one was open for 10% of the time, Pallas kernels for 0%

profile of v1, /device:TPU:2, one launch (start us, length us, event | category | flops | bytes accessed | tf_op | source)
XLA Modules:
  0.0 377.2 jit_solution(908125450925536559)
XLA Ops:
  7.2 0.8 slice_bitcast_fusion.3
  8.0 0.8 stack.2
  8.8 9.2 %all-to-all-start = ((bf16[16,1,3,2816]{3,2,1,0:T(4,128)(2,1)}), bf16[16,1,3,2816]{3,2,1,0:T(4,128)(2,1)S(1)}, u32[]{:S(2)}, u32[]{:S(2)}) async-start(bf16[16,1,3,2816]{3,2,1,0:T(4,128)(2,1)} %stack.2), calls=%async_computation | async-start | bytes 720896 | tf_op jit(solution)/shard_map/all_to_all | solution.py:52
  18.1 0.7 neg.23
  18.8 23.8 %all-gather = bf16[4096,40]{0,1:T(8,128)(2,1)S(1)} all-gather(bf16[256,40]{0,1:T(8,128)(2,1)} %param.17), channel_id=2, replica_groups=mesh['dp'=32,'seq'=16] {'seq'}, dimensions={0}, use_global_device_ids=true | all-gather | bytes 348160 | tf_op jit(solution)/shard_map/all_gather | solution.py:54
  42.6 0.8 multiply_bitcast_fusion
  43.4 0.6 reduce-window.11
  44.0 0.2 slice_reduce_fusion
  44.2 1.2 dynamic_slice.62
  46.1 0.8 reduce-window.10
  47.0 1.1 slice_reduce_fusion.5
  48.7 0.7 fusion.55
  49.5 0.6 slice.93
  50.1 0.2 copy.93
  50.3 0.6 fusion.30
  50.9 0.2 fusion.45
  51.4 0.8 fusion.42
  52.1 0.1 broadcast.164
  52.3 0.1 add_bitcast_fusion
  52.4 0.6 slice_reduce_fusion.1
  53.7 0.6 broadcast_compare_fusion.1
  54.3 0.1 fusion.38
  54.4 0.2 convert_reduce_fusion.2
  55.2 0.2 broadcast_in_dim.178
  55.4 2.1 copy.73
  57.5 0.2 broadcast_in_dim.184
  57.8 2.1 copy.78
  60.0 0.2 fusion.32
  60.2 5.9 %multiply_convert_fusion.2 = bf16[1,256,2816]{2,1,0:T(8,128)(2,1)S(1)} fusion(bf16[256,2816]{1,0:T(8,128)(2,1)} %param.15, bf16[1,3,2816]{2,1,0:T(4,128)(2,1)S(1)} %copy.108, bf16[1,256,2816]{2,1,0:T(8,128)(2,1)} %bitcast.156, f32[2816]{0:T(1024)S(1)} %get-tuple-element.357, f32[256]{0:T(256)S(1)} %bitcast.177, f32[2816]{0:T(1024)S(1)} %get-tuple-element.358, ...), kind=kLoop, calls=%fused_computation.33 | loop fusion | flops 20905984 | bytes 4401664 | tf_op jit(solution)/shard_map/convert_element_type | solution.py:88
  66.1 2.6 fusion.17
  68.7 0.4 copy-done
  69.1 1.9 fusion.25
  71.0 0.2 reduce-scatter.2.cloned.1.call-start
  71.4 0.7 compare_and_fusion
  72.0 0.2 fusion.28
  72.3 1.4 copy.74
  73.7 146.0 %all-gather.4.cloned.1.call-done = f32[40960,128]{1,0:T(8,128)} async-done(((f32[2560,128]{1,0:T(8,128)}), f32[40960,128]{1,0:T(8,128)}) %all-gather.4.cloned.1.call-update) | async-done | bytes 20971536 | tf_op jit(solution)/shard_map/all_gather | solution.py:112
  219.8 38.9 %fusion.6 = f32[2560,1,128]{2,1,0:T(1,128)S(1)} fusion(f32[16,2560,1]{0,2,1:T(1,128)S(1)} %bitcast.154, f32[16,2560,128]{2,1,0:T(8,128)} %bitcast.150), kind=kOutput, calls=%fused_computation.15 | convolution fusion | flops 62914560 | bytes 22446080 | tf_op jit(solution)/shard_map/ick,ckn->ikn/dot_general | solution.py:109
  258.7 20.2 %while.17 = (s32[]{:T(128)}, bf16[3,2560,128]{2,1,0:T(8,128)(2,1)}, s32[3]{0:T(128)S(1)}, s32[3]{0:T(128)S(1)}, s32[1]{0:T(128)}, /*index=5*/bf16[1,256,2560]{1,...) while((s32[]{:T(128)}, bf16[3,2560,128]{2,1,0:T(8,128)(2,1)}, ...), condition=%wide.region_13.14_spmd, body=%wide.region_10.13_spmd.sunk | while | flops 170742112 | bytes 7442075 | solution.py:184
  258.7 0.6 dynamic_slice.66
  261.2 0.6 dynamic_slice.67
  263.1 4.0 %conditional.2 = (bf16[1,2560,128]{2,1,0:T(8,128)(2,1)S(1)}) conditional(s32[]{:T(128)} %bitcast.146, () %tuple.66, (bf16[1,256,2560]{1,2,0:T(8,128)(2,1)}, s32[]{:T(128)}, s32[1,256]{1,0:T(1,128)S(1)}, s32[]{:T(128)}, s32[]{:T(128)}, /*index=5*/f32[1,256,40]{1,2,0:T(8,128)S(1)}, bf16[1,256,128]{2,1,0:T(8,128)(2,1)S(1)}, s32[1]{0:T(128)}, ...), branch_computations={%region_11.11_spmd, %region_12.12_spmd} | conditional | flops 170742096 | bytes 6130356 | solution.py:182
  263.1 0.2 dynamic-slice_reduce_fusion
  263.3 0.7 compare_reduce_fusion
  264.1 1.7 fusion.1
  266.6 0.5 fusion
  267.1 0.9 constant_dynamic-update-slice_fusion.2
  268.0 0.6 dynamic_slice.66
  270.5 0.6 dynamic_slice.67
  272.4 0.1 conditional.2
  272.5 0.9 constant_dynamic-update-slice_fusion.2
  273.4 0.6 dynamic_slice.66
  275.9 0.6 dynamic_slice.67
  277.8 0.1 conditional.2
  277.9 0.9 constant_dynamic-update-slice_fusion.2
  279.0 1.7 broadcast_in_dim.192
  280.7 3.2 copy.79
  284.2 1.1 fusion.36
  285.3 5.1 %fusion.8 = f32[40,64,256]{2,1,0:T(8,128)} fusion(bf16[256,40,64]{0,2,1:T(8,128)(2,1)} %bitcast.30, f32[40,256]{1,0:T(8,128)S(1)} %bitcast.157, f32[256,256]{1,0:T(8,128)S(1)} %fusion.36, pred[256,256]{1,0:T(8,128)(4,1)S(1)} %fusion.34), kind=kOutput, calls=%fused_computation.18 | convolution fusion | flops 346030080 | bytes 4300800 | tf_op jit(solution)/shard_map/while/body/eval_jaxpr/hts,shp->thp/dot_general | solution.py:126
  290.3 3.4 copy.80
  293.7 4.6 %multiply_reduce_fusion = (f32[256]{0:T(256)S(1)}, f32[256,2560]{1,0:T(8,128)S(1)}) fusion(bf16[256,2560]{1,0:T(8,128)(2,1)S(1)} %copy-done.7, f32[2560]{0:T(1024)S(1)} %mul.239, bf16[1,256,2816]{2,1,0:T(8,128)(2,1)} %copy-done.1, f32[256,2560]{1,0:T(8,128)} %copy.80, f32[256,2560]{1,0:T(8,128)} %copy.79, f32[2560,128]{1,0:T(8,128)S(1)} %bitcast.149), kind=kOutput, calls=%fused_computation.40 | convolution fusion | flops 176619264 | bytes 11873280 | tf_op jit(solution)/shard_map/while/body/eval_jaxpr/dot_general | solution.py:132
  298.3 1.3 multiply_convert_fusion.3
  299.7 69.0 %reduce-scatter.2.cloned.1.call-done = bf16[160,3,128]{2,0,1:T(8,128)(2,1)} async-done(((bf16[2560,3,128]{2,0,1:T(8,128)(2,1)}), bf16[160,3,128]{2,0,1:T(8,128)(2,1)}) %reduce-scatter.2.cloned.1.call-update) | async-done | bytes 122896 | tf_op jit(solution)/shard_map/reduce_scatter | solution.py:185
  368.7 1.6 convert_bitcast_fusion.2
  (51 shorter events, 1.6 us)
Async XLA Ops:
  7.2 43.2 %copy-start.5 = (f32[40]{0:T(128)S(1)}, f32[40]{0:T(128)}, u32[]{:S(2)}) copy-start(f32[40]{0:T(128)} %param.22) | copy-start | bytes 484
  7.2 43.8 %copy-start.4 = (s32[16]{0:T(128)S(1)}, s32[16]{0:T(128)}, u32[]{:S(2)}) copy-start(s32[16]{0:T(128)} %param.19) | copy-start | bytes 196
  8.8 51.1 %all-to-all-start = ((bf16[16,1,3,2816]{3,2,1,0:T(4,128)(2,1)}), bf16[16,1,3,2816]{3,2,1,0:T(4,128)(2,1)S(1)}, u32[]{:S(2)}, u32[]{:S(2)}) async-start(bf16[16,1,3,2816]{3,2,1,0:T(4,128)(2,1)} %stack.2), calls=%async_computation | async-start | bytes 720896 | tf_op jit(solution)/shard_map/all_to_all | solution.py:52
  18.1 201.7 %all-gather.4.cloned.1.call-start = ((), (), s32[]{:S(2)}) async-start(), calls=%async_computation.3 | async-start | bytes 22282240 | tf_op jit(solution)/shard_map/all_gather | solution.py:112
  57.7 2.4 copy-start.3
  66.1 153.7 %copy-start.1 = (bf16[1,256,2816]{2,1,0:T(8,128)(2,1)}, bf16[1,256,2816]{2,1,0:T(8,128)(2,1)S(1)}, u32[]{:S(2)}) copy-start(bf16[1,256,2816]{2,1,0:T(8,128)(2,1)S(1)} %multiply_convert_fusion.2) | copy-start | bytes 4325380
  66.1 3.0 copy-start
  71.0 297.7 %reduce-scatter.2.cloned.1.call-start = ((), (), s32[]{:S(2)}) async-start(), calls=%async_computation.2 | async-start | bytes 2088960 | tf_op jit(solution)/shard_map/reduce_scatter | solution.py:185
  280.7 3.2 copy-start.6
  290.3 3.4 copy-start.7
  293.7 4.6 %copy-start.2 = (f32[2560]{0:T(1024)S(1)}, f32[2560]{0:T(1024)}, u32[]{:S(2)}) copy-start(f32[2560]{0:T(1024)} %param.25) | copy-start | bytes 30724
Sparse Core Ops, SparseCore 0:
  71.1 148.5 all-gather.3
  279.0 89.6 reduce-scatter.1
